TPU v7x, 512 devices: a whole 4x4x16 slice. The times are simulated.
512 devices in a mesh: comp: 32 (over z, core), feat: 16 (over x, y).
Axes of the slice: x: 4, y: 4, z: 16, core: 2. Of those that a mesh axis runs over, the one named last changes fastest.
Arguments:
- block_values: bfloat16 [32, 16, 24, 128, 128], P('comp', 'feat'), may hold values from -0.0625 to 0.0625
- block_rows: int32 [32, 16, 24], P('comp', 'feat'), may hold values from 0 to 15, as said below
- block_cols: int32 [32, 16, 24], P('comp', 'feat'), may hold values from 0 to 13, as said below
- block_counts: int32 [32, 16], P('comp', 'feat'), may hold values from 8 to 24, as said below
- right_side: float32 [65536, 128], P(('comp', 'feat')), may hold values from -6 to 6
- ridge: float32 [128], replicated, may hold values from 0.1 to 2
Outputs:
- solution: float32 [28672, 128], P('feat')
- residual: float32 [65536, 128], P(('comp', 'feat'))
Inputs may be any that keep to these rules, and one draw needn't show every extreme that they name: Within one device the listed (block_rows, block_cols) pairs of all 24 slots are distinct; block rows are very uneven in how many blocks they hold. `block_cols`: see block_rows. `block_counts`: slots at or beyond a device's count are ignored; some device is full in every draw.
All inputs are finite; a program needn't handle non-finite values.
Results may differ from a plain program's by a relative error of at most 0.0029.
Values may be sent and summed in bfloat16 or wider, within the bound.
No kernel may reach another device: no remote copies, remote signals or barrier semaphores. Data moves between devices by JAX's collectives and lax.ppermute only.
A program may use at most 64 MiB of HBM per device.

v0:
```python
import jax
import jax.numpy as jnp
from jax import lax
from jax.sharding import PartitionSpec as P

RB_DEV = 16
CB_DEV = 14
ITERS = 2


def reduce_over(partial, axis, parts):
    rows = partial.shape[0] // parts
    pieces = partial.reshape(parts, rows, *partial.shape[1:])
    return lax.all_to_all(pieces, axis, 0, 0, tiled=True).sum(0)


def total_over_mesh(stacked, n_comp, n_feat):
    spread = jnp.broadcast_to(stacked[None], (n_feat,) + stacked.shape)
    by_feat = lax.all_to_all(spread, "feat", 0, 0, tiled=True).sum(0)
    spread = jnp.broadcast_to(by_feat[None], (n_comp,) + stacked.shape)
    return lax.all_to_all(spread, "comp", 0, 0, tiled=True).sum(0)


def shards(block_values, block_rows, block_cols, block_counts, right_side, ridge, n_comp, n_feat):
    values = block_values[0, 0]
    slot_rows = block_rows[0, 0]
    slot_cols = block_cols[0, 0]
    count_of_slots = block_counts[0, 0]
    responses = right_side.shape[1]
    total_slot_number = values.shape[0]
    block_edge = values.shape[1]
    feat_rows = CB_DEV * block_edge
    own_rows = feat_rows // n_comp
    comp_index = lax.axis_index("comp")
    slot_live = (jnp.arange(total_slot_number) < count_of_slots).astype(jnp.float32)
    row_lookup_table = (jnp.arange(RB_DEV)[:, None] == slot_rows[None, :]).astype(
        jnp.float32
    ) * slot_live[None, :]
    col_table = (jnp.arange(CB_DEV)[:, None] == slot_cols[None, :]).astype(jnp.float32) * slot_live[
        None, :
    ]

    def backward(low_slab):
        row_slabs = low_slab.reshape(RB_DEV, block_edge, responses)
        selected = jnp.take(row_slabs, slot_rows, axis=0)
        block_products = jnp.einsum(
            "sij,sik->sjk", values, selected, preferred_element_type=jnp.float32
        )
        summed = jnp.einsum(
            "qs,sjk->qjk", col_table, block_products, precision=lax.Precision.HIGHEST
        )
        return summed.reshape(feat_rows, responses)

    def forward(direction):
        col_panels = direction.astype(jnp.bfloat16).reshape(CB_DEV, block_edge, responses)
        forward_selected = jnp.take(col_panels, slot_cols, axis=0)
        forward_block_products = jnp.einsum(
            "sij,sjk->sik", values, forward_selected, preferred_element_type=jnp.float32
        )
        forward_summed = jnp.einsum(
            "rs,sik->rik", row_lookup_table, forward_block_products, precision=lax.Precision.HIGHEST
        )
        return reduce_over(forward_summed.reshape(RB_DEV * block_edge, responses), "feat", n_feat)

    def slab_of(current):
        return lax.all_gather(current.astype(jnp.bfloat16), "feat", axis=0, tiled=True)

    def gradient_rows(current):
        return reduce_over(backward(slab_of(current)), "comp", n_comp)

    def own_part(full):
        return lax.dynamic_slice_in_dim(full, comp_index * own_rows, own_rows, axis=0)

    def col_sq(x):
        return jnp.sum(x * x, axis=0)

    residual = right_side
    gradient_own = gradient_rows(residual)
    direction = lax.all_gather(gradient_own, "comp", axis=0, tiled=True)
    image_rows = forward(direction)
    energy, image_energy = total_over_mesh(
        jnp.stack([col_sq(gradient_own), col_sq(image_rows)]), n_comp, n_feat
    )
    step_size = energy / (image_energy + ridge * energy)
    solution = step_size * direction
    residual = residual - step_size * image_rows
    for _ in range(1, ITERS):
        gradient_own = gradient_rows(residual) - ridge * own_part(solution)
        gathered = lax.all_gather(
            jnp.concatenate([gradient_own, col_sq(gradient_own)[None]], axis=0),
            "comp",
            axis=0,
            tiled=False,
        )
        gradient = gathered[:, :own_rows].reshape(feat_rows, responses)
        comp_energy = jnp.sum(gathered[:, own_rows], axis=0)
        spread = jnp.broadcast_to(comp_energy[None, None], (n_feat, 1, responses))
        next_energy = lax.all_to_all(spread, "feat", 0, 0, tiled=True).sum(0)[0]
        direction = gradient + next_energy / energy * direction
        energy = next_energy
        image_rows = forward(direction)
        image_energy, direction_energy = total_over_mesh(
            jnp.stack([col_sq(image_rows), col_sq(own_part(direction))]), n_comp, n_feat
        )
        step_size = energy / (image_energy + ridge * direction_energy)
        solution = solution + step_size * direction
        residual = residual - step_size * image_rows
    return (solution, residual)


def solution(mesh):
    placed = (
        P("comp", "feat", None, None, None),
        P("comp", "feat", None),
        P("comp", "feat", None),
        P("comp", "feat"),
        P(("comp", "feat"), None),
        P(),
    )
    n_comp = mesh.shape["comp"]
    n_feat = mesh.shape["feat"]

    def body(*args):
        return shards(*args, n_comp=n_comp, n_feat=n_feat)

    return jax.shard_map(
        body,
        mesh=mesh,
        in_specs=placed,
        out_specs=(P("feat", None), P(("comp", "feat"), None)),
        check_vma=False,
    )
```

profile of v0, /device:TPU:1, one launch (start us, length us, event | category | flops | bytes accessed | tf_op | source)
XLA Modules:
  0.0 376.8 jit_solution(10062302333413157449)
XLA Ops:
  0.6 0.0 copy-start
  0.6 0.7 compare_and_fusion.1
  1.4 0.7 compare_select_fusion.1
  2.7 0.8 convert_element_type.22
  3.6 20.0 %all_gather.15 = bf16[2048,128]{1,0:T(8,128)(2,1)S(1)} all-gather(bf16[128,128]{1,0:T(8,128)(2,1)S(1)} %convert_element_type.22), channel_id=1, replica_groups=mesh['comp'=32,'feat'=16] {'feat'}, dimensions={0}, use_global_device_ids=true | all-gather | bytes 557056 | tf_op jit(solution)/shard_map/all_gather | solution.py:66
  23.5 0.7 gather_fusion
  24.2 0.0 copy-done
  24.2 1.7 convolution_bitcast_fusion.3
  25.9 0.0 copy-start.3
  25.9 2.0 copy.43
  27.9 0.0 copy-done.3
  27.9 1.0 fusion.25
  28.9 1.2 copy.44
  30.1 21.0 %all-to-all-start = ((f32[32,56,128]{2,1,0:T(8,128)}), f32[32,56,128]{2,1,0:T(8,128)S(1)}, u32[]{:S(2)}, u32[]{:S(2)}) async-start(f32[32,56,128]{2,1,0:T(8,128)} %bitcast.7), calls=%async_computation | async-start | bytes 1835008 | tf_op jit(solution)/shard_map/all_to_all | solution.py:14
  51.2 50.2 %all-to-all-done = f32[32,56,128]{2,1,0:T(8,128)S(1)} async-done(((f32[32,56,128]{2,1,0:T(8,128)}), f32[32,56,128]{2,1,0:T(8,128)S(1)}, u32[]{:S(2)}, u32[]{:S(2)}) %all-to-all-start) | async-done | bytes 917536 | tf_op jit(solution)/shard_map/all_to_all | solution.py:14
  101.4 0.1 reduce_sum.137
  101.4 29.7 %all_gather.16 = f32[1792,128]{1,0:T(8,128)S(1)} all-gather(f32[56,128]{1,0:T(8,128)S(1)} %reduce_sum.137), channel_id=1, replica_groups=mesh['comp'=32,'feat'=16] {'comp'}, dimensions={0}, use_global_device_ids=true | all-gather | bytes 946176 | tf_op jit(solution)/shard_map/all_gather | solution.py:79
  131.2 0.7 gather_fusion.1
  131.9 2.0 convolution_bitcast_fusion.2
  133.9 0.0 copy-start.4
  133.9 2.0 copy.46
  135.9 0.0 copy-done.4
  135.9 1.0 fusion.19
  136.9 1.3 copy.47
  138.2 0.0 copy-start.2
  138.2 0.0 copy-start.1
  138.2 4.8 %all-to-all-start.1 = ((f32[16,128,128]{2,1,0:T(8,128)}), f32[16,128,128]{2,1,0:T(8,128)S(1)}, u32[]{:S(2)}, u32[]{:S(2)}) async-start(f32[16,128,128]{2,1,0:T(8,128)} %copy.47), calls=%async_computation.1 | async-start | bytes 2097152 | tf_op jit(solution)/shard_map/all_to_all | solution.py:14
  143.1 16.0 %all-to-all-done.1 = f32[16,128,128]{2,1,0:T(8,128)S(1)} async-done(((f32[16,128,128]{2,1,0:T(8,128)}), f32[16,128,128]{2,1,0:T(8,128)S(1)}, u32[]{:S(2)}, u32[]{:S(2)}) %all-to-all-start.1) | async-done | bytes 1048608 | tf_op jit(solution)/shard_map/all_to_all | solution.py:14
  159.1 0.1 reduce_sum.139
  159.2 10.6 %all_to_all.45 = f32[16,2,128]{2,1,0:T(2,128)S(1)} all-to-all(f32[16,2,128]{2,1,0:T(2,128)S(1)} %broadcast_in_dim.30), channel_id=1, replica_groups=mesh['comp'=32,'feat'=16] {'feat'}, dimensions={0} | all-to-all | bytes 32768 | tf_op jit(solution)/shard_map/all_to_all | solution.py:19
  169.9 19.7 %all_to_all.46 = f32[32,2,128]{2,1,0:T(2,128)S(1)} all-to-all(f32[32,2,128]{2,1,0:T(2,128)S(1)} %broadcast_in_dim.31), channel_id=1, replica_groups=mesh['comp'=32,'feat'=16] {'comp'}, dimensions={0} | all-to-all | bytes 65536 | tf_op jit(solution)/shard_map/all_to_all | solution.py:21
  189.6 0.0 copy-done.2
  189.6 0.0 copy-done.1
  189.6 16.7 %all_gather.17 = bf16[2048,128]{1,0:T(8,128)(2,1)S(1)} all-gather(bf16[128,128]{1,0:T(8,128)(2,1)S(1)} %fusion.16), channel_id=1, replica_groups=mesh['comp'=32,'feat'=16] {'feat'}, dimensions={0}, use_global_device_ids=true | all-gather | bytes 557056 | tf_op jit(solution)/shard_map/all_gather | solution.py:66
  206.3 0.7 gather_fusion.2
  207.0 1.7 convolution_bitcast_fusion.1
  208.7 2.0 copy.51
  210.6 1.0 fusion.23
  211.7 1.2 copy.52
  212.9 10.1 %all-to-all-start.4 = ((f32[32,56,128]{2,1,0:T(8,128)}), f32[32,56,128]{2,1,0:T(8,128)S(1)}, u32[]{:S(2)}, u32[]{:S(2)}) async-start(f32[32,56,128]{2,1,0:T(8,128)} %bitcast.17), calls=%async_computation.4 | async-start | bytes 1835008 | tf_op jit(solution)/shard_map/all_to_all | solution.py:14
  223.0 1.0 broadcast_multiply_fusion
  224.0 49.3 %all-to-all-done.4 = f32[32,56,128]{2,1,0:T(8,128)S(1)} async-done(((f32[32,56,128]{2,1,0:T(8,128)}), f32[32,56,128]{2,1,0:T(8,128)S(1)}, u32[]{:S(2)}, u32[]{:S(2)}) %all-to-all-start.4) | async-done | bytes 917536 | tf_op jit(solution)/shard_map/all_to_all | solution.py:14
  273.3 0.1 reduce_sum.143
  273.3 0.8 multiply_reduce_fusion.3
  274.1 30.6 %all-gather.1 = f32[32,57,128]{2,1,0:T(8,128)S(1)} all-gather(f32[1,57,128]{2,1,0:T(8,128)S(1)} %maximum_bitcast_fusion), channel_id=2, replica_groups=mesh['comp'=32,'feat'=16] {'comp'}, dimensions={0}, use_global_device_ids=true | all-gather | bytes 963072 | tf_op jit(solution)/shard_map/all_gather | solution.py:89
  304.7 0.1 slice_reduce_fusion
  304.8 0.6 broadcast_in_dim.33
  305.4 4.0 %all-to-all-start.5 = ((f32[16,1,128]{2,1,0:T(1,128)}), f32[16,1,128]{2,1,0:T(1,128)S(1)}, u32[]{:S(2)}, u32[]{:S(2)}) async-start(f32[16,1,128]{2,1,0:T(1,128)} %broadcast_in_dim.33), calls=%async_computation.5 | async-start | bytes 16384 | tf_op jit(solution)/shard_map/all_to_all | solution.py:98
  309.4 1.0 slice.17
  310.4 5.3 %all-to-all-done.5 = f32[16,1,128]{2,1,0:T(1,128)S(1)} async-done(((f32[16,1,128]{2,1,0:T(1,128)}), f32[16,1,128]{2,1,0:T(1,128)S(1)}, u32[]{:S(2)}, u32[]{:S(2)}) %all-to-all-start.5) | async-done | bytes 8224 | tf_op jit(solution)/shard_map/all_to_all | solution.py:98
  315.8 2.2 fusion.53
  318.0 0.7 gather_fusion.3
  318.7 2.0 convolution_bitcast_fusion
  320.7 2.0 copy.55
  322.7 1.0 fusion.17
  323.7 1.3 copy.56
  325.0 3.7 all-to-all-start.6
  328.7 0.8 multiply_reduce_fusion.2
  329.4 14.4 %all-to-all-done.6 = f32[16,128,128]{2,1,0:T(8,128)S(1)} async-done(((f32[16,128,128]{2,1,0:T(8,128)}), f32[16,128,128]{2,1,0:T(8,128)S(1)}, u32[]{:S(2)}, u32[]{:S(2)}) %all-to-all-start.6) | async-done | bytes 1048608 | tf_op jit(solution)/shard_map/all_to_all | solution.py:14
  343.9 0.1 reduce_sum.148
  344.0 10.1 %all_to_all.47 = f32[16,2,128]{2,1,0:T(2,128)S(1)} all-to-all(f32[16,2,128]{2,1,0:T(2,128)S(1)} %broadcast_in_dim.34), channel_id=1, replica_groups=mesh['comp'=32,'feat'=16] {'feat'}, dimensions={0} | all-to-all | bytes 32768 | tf_op jit(solution)/shard_map/all_to_all | solution.py:19
  354.2 19.7 %all_to_all.48 = f32[32,2,128]{2,1,0:T(2,128)S(1)} all-to-all(f32[32,2,128]{2,1,0:T(2,128)S(1)} %broadcast_in_dim.35), channel_id=1, replica_groups=mesh['comp'=32,'feat'=16] {'comp'}, dimensions={0} | all-to-all | bytes 65536 | tf_op jit(solution)/shard_map/all_to_all | solution.py:21
  374.0 2.2 multiply_add_fusion
  376.2 0.6 multiply_subtract_fusion
  (25 shorter events, 0.4 us)
Async XLA Ops:
  0.6 23.6 %copy-start = (bf16[1,1,24,128,128]{4,3,2,1,0:T(8,128)(2,1)S(1)}, bf16[1,1,24,128,128]{4,3,2,1,0:T(8,128)(2,1)}, u32[]{:S(2)}) copy-start(bf16[1,1,24,128,128]{4,3,2,1,0:T(8,128)(2,1)} %param.10) | copy-start | bytes 2359300
  25.9 2.0 copy-start.3
  30.1 71.2 %all-to-all-start = ((f32[32,56,128]{2,1,0:T(8,128)}), f32[32,56,128]{2,1,0:T(8,128)S(1)}, u32[]{:S(2)}, u32[]{:S(2)}) async-start(f32[32,56,128]{2,1,0:T(8,128)} %bitcast.7), calls=%async_computation | async-start | bytes 1835008 | tf_op jit(solution)/shard_map/all_to_all | solution.py:14
  133.9 2.0 copy-start.4
  138.2 51.4 %copy-start.2 = (f32[128]{0:T(128)S(1)}, f32[128]{0:T(128)}, u32[]{:S(2)}) copy-start(f32[128]{0:T(128)} %param.15) | copy-start | bytes 1540
  138.2 51.4 %copy-start.1 = (f32[128,128]{1,0:T(8,128)S(1)}, f32[128,128]{1,0:T(8,128)}, u32[]{:S(2)}) copy-start(f32[128,128]{1,0:T(8,128)} %param.14) | copy-start | bytes 196612
  138.2 20.9 %all-to-all-start.1 = ((f32[16,128,128]{2,1,0:T(8,128)}), f32[16,128,128]{2,1,0:T(8,128)S(1)}, u32[]{:S(2)}, u32[]{:S(2)}) async-start(f32[16,128,128]{2,1,0:T(8,128)} %copy.47), calls=%async_computation.1 | async-start | bytes 2097152 | tf_op jit(solution)/shard_map/all_to_all | solution.py:14
  212.9 60.4 %all-to-all-start.4 = ((f32[32,56,128]{2,1,0:T(8,128)}), f32[32,56,128]{2,1,0:T(8,128)S(1)}, u32[]{:S(2)}, u32[]{:S(2)}) async-start(f32[32,56,128]{2,1,0:T(8,128)} %bitcast.17), calls=%async_computation.4 | async-start | bytes 1835008 | tf_op jit(solution)/shard_map/all_to_all | solution.py:14
  305.4 10.4 %all-to-all-start.5 = ((f32[16,1,128]{2,1,0:T(1,128)}), f32[16,1,128]{2,1,0:T(1,128)S(1)}, u32[]{:S(2)}, u32[]{:S(2)}) async-start(f32[16,1,128]{2,1,0:T(1,128)} %broadcast_in_dim.33), calls=%async_computation.5 | async-start | bytes 16384 | tf_op jit(solution)/shard_map/all_to_all | solution.py:98
  325.0 18.9 %all-to-all-start.6 = ((f32[16,128,128]{2,1,0:T(8,128)}), f32[16,128,128]{2,1,0:T(8,128)S(1)}, u32[]{:S(2)}, u32[]{:S(2)}) async-start(f32[16,128,128]{2,1,0:T(8,128)} %copy.56), calls=%async_computation.6 | async-start | bytes 2097152 | tf_op jit(solution)/shard_map/all_to_all | solution.py:14
where the time goes:
time: 378 us; the launch traced here: 377 us
  blocking collectives  157 us (42%)
  waiting for transfers between devices  135 us (36%)
  starting transfers between devices  43.7 us (12%)
  local copies, waits for them, and re-layouts  17.3 us (5%)
  matrix products  11.4 us (3%)
  other arithmetic  10.5 us (3%)
    all_to_all x4, waiting for transfers between devices, reduce_over(): return lax.all_to_all(pieces, axis, 0, 0, tiled=True).sum(0)  130 us
    all_to_all x4, starting transfers between devices, reduce_over(): return lax.all_to_all(pieces, axis, 0, 0, tiled=True).sum(0)  39.6 us
    all_to_all x2, blocking collectives, total_over_mesh(): return lax.all_to_all(spread, 'comp', 0, 0, tiled=True).sum(0)  39.4 us
    all_gather x2, blocking collectives, slab_of(): lax.all_gather(current.astype(jnp.bfloat16), 'feat', axis=0, tiled=True)  36.6 us
    all_gather x1, blocking collectives, shards(): lax.all_gather(jnp.concatenate([gradient_own, col_sq(gradient_own)[None]]...  30.6 us
    all_gather x1, blocking collectives, shards(): direction = lax.all_gather(gradient_own, 'comp', axis=0, tiled=True)  29.7 us
    all_to_all x2, blocking collectives, total_over_mesh(): by_feat = lax.all_to_all(spread, 'feat', 0, 0, tiled=True).sum(0)  20.8 us
  transfers between devices with their start and end apart: 5, of which 5 were waited for; matrix products, arithmetic and copies ran while one was open for 1% of the time, Pallas kernels for 0%

commit v1 on v0

--- a/solution.py
+++ b/solution.py
@@ -1,3 +1,4 @@
+import functools
 import jax
 import jax.numpy as jnp
 from jax import lax
@@ -6,6 +7,36 @@
 RB_DEV = 16
 CB_DEV = 14
 ITERS = 2
+
+
+def wrap_routes_all(mat, peer_axis):
+    prior = lax.axis_size(peer_axis)
+    y1, before, side_arr = (prior, lax.axis_index(peer_axis), mat.shape[0])
+    rack = [w * y1 if num == 0 else w for num, w in enumerate(mat.shape)]
+    view_out = u_next = mat
+    even = lax.dynamic_update_slice_in_dim(
+        jnp.zeros(rack, mat.dtype), mat, before * side_arr, axis=0
+    )
+    idx = 1
+    while idx < y1 // 2 + 1:
+        view_out = lax.ppermute(
+            view_out, axis_name=peer_axis, perm=[(num, (num + 1) % y1) for num in range(y1)]
+        )
+        even = lax.dynamic_update_slice_in_dim(
+            even, view_out, (before - idx) % y1 * side_arr, axis=0
+        )
+        if 2 * idx < y1:
+            u_next = lax.ppermute(
+                u_next, axis_name=peer_axis, perm=[(num, (num - 1) % y1) for num in range(y1)]
+            )
+            even = lax.dynamic_update_slice_in_dim(
+                even, u_next, (before + idx) % y1 * side_arr, axis=0
+            )
+        idx = idx + 1
+    return even
+
+
+cover_spans = functools.partial(wrap_routes_all, peer_axis="feat")
 
 
 def reduce_over(partial, axis, parts):
@@ -63,7 +94,7 @@
         return reduce_over(forward_summed.reshape(RB_DEV * block_edge, responses), "feat", n_feat)
 
     def slab_of(current):
-        return lax.all_gather(current.astype(jnp.bfloat16), "feat", axis=0, tiled=True)
+        return cover_spans(current.astype(jnp.bfloat16))
 
     def gradient_rows(current):
         return reduce_over(backward(slab_of(current)), "comp", n_comp)

time: 378 us -> 479 us (1.27)
  starting transfers between devices: 43.7 us -> 167 us
  blocking collectives: 157 us -> 119 us
  waiting for transfers between devices: 135 us -> 148 us
    ppermute x0 -> x30, starting transfers between devices: none -> 125 us  [the longest x14 92.1 us: wrap_routes_all(): lax.ppermute(u_next, axis_name=peer_axis, perm=[(num, (num - 1) % y1) for...]
    all_gather x2 -> x0, blocking collectives: 36.6 us -> none  [slab_of(): lax.all_gather(current.astype(jnp.bfloat16), 'feat', axis=0, tiled=True)]
    ppermute x0 -> x30, waiting for transfers between devices: none -> 11.9 us  [the longest x16 11.9 us: wrap_routes_all(): lax.ppermute(view_out, axis_name=peer_axis, perm=[(num, (num + 1) % y1) f...]
  transfers between devices with their start and end apart: 5 -> 35, of which waited for: 5 -> 7; matrix products, arithmetic and copies ran while one was open for 1% -> 1% of each run, Pallas kernels for 0% -> 0%
where the time goes in v1:
time: 479 us; the launch traced here: 477 us
  starting transfers between devices  167 us (35%)
  waiting for transfers between devices  148 us (31%)
  blocking collectives  119 us (25%)
  local copies, waits for them, and re-layouts  17.9 us (4%)
  matrix products  11.4 us (2%)
  other arithmetic  10.6 us (2%)
    all_to_all x4, waiting for transfers between devices, reduce_over(): return lax.all_to_all(pieces, axis, 0, 0, tiled=True).sum(0)  131 us
    ppermute x14, starting transfers between devices, wrap_routes_all(): lax.ppermute(u_next, axis_name=peer_axis, perm=[(num, (num - 1) % y1) for...  92.1 us
    all_to_all x2, blocking collectives, total_over_mesh(): return lax.all_to_all(spread, 'comp', 0, 0, tiled=True).sum(0)  39.1 us
    all_to_all x4, starting transfers between devices, reduce_over(): return lax.all_to_all(pieces, axis, 0, 0, tiled=True).sum(0)  38 us
    ppermute x16, starting transfers between devices, wrap_routes_all(): lax.ppermute(view_out, axis_name=peer_axis, perm=[(num, (num + 1) % y1) f...  33.3 us
    all_gather x1, blocking collectives, shards(): lax.all_gather(jnp.concatenate([gradient_own, col_sq(gradient_own)[None]]...  30.6 us
    all_gather x1, blocking collectives, shards(): direction = lax.all_gather(gradient_own, 'comp', axis=0, tiled=True)  29.7 us
    all_to_all x2, blocking collectives, total_over_mesh(): by_feat = lax.all_to_all(spread, 'feat', 0, 0, tiled=True).sum(0)  19.7 us
  transfers between devices with their start and end apart: 35, of which 7 were waited for; matrix products, arithmetic and copies ran while one was open for 1% of the time, Pallas kernels for 0%

profile of v1, /device:TPU:1, one launch (start us, length us, event | category | flops | bytes accessed | tf_op | source)
XLA Modules:
  0.0 476.8 jit_solution(12586926922955454531)
XLA Ops:
  1.6 4.0 collective-permute-start
  5.7 5.6 %collective-permute-start.1 = (bf16[128,128]{1,0:T(8,128)(2,1)S(1)}, bf16[128,128]{1,0:T(8,128)(2,1)S(1)}, u32[]{:S(2)}, u32[]{:S(2)}) collective-permute-start(bf16[128,128]{1,0:T(8,128)(2,1)S(1)} %get-tuple-element.11), channel_id=1, source_target_pairs={{0,15},{1,0},{2,1},{3,2},{4,3},{5,4},{6,5},{7,6},{8,7},{9,8},{10,9... | collective-permute-start | bytes 98312 | tf_op jit(solution)/shard_map/ppermute | solution.py:29
  13.5 1.9 collective-permute-start.2
  15.5 6.7 %collective-permute-start.3 = (bf16[128,128]{1,0:T(8,128)(2,1)S(1)}, bf16[128,128]{1,0:T(8,128)(2,1)S(1)}, u32[]{:S(2)}, u32[]{:S(2)}) collective-permute-start(bf16[128,128]{1,0:T(8,128)(2,1)S(1)} %collective-permute-done.1), channel_id=1, source_target_pairs={{0,15},{1,0},{2,1},{3,2},{4,3},{5,4},{6,5},{7,6},{8,7},{9,8},{10,9... | collective-permute-start | bytes 98312 | tf_op jit(solution)/shard_map/ppermute | solution.py:29
  22.2 1.9 collective-permute-start.4
  24.2 6.7 %collective-permute-start.5 = (bf16[128,128]{1,0:T(8,128)(2,1)S(1)}, bf16[128,128]{1,0:T(8,128)(2,1)S(1)}, u32[]{:S(2)}, u32[]{:S(2)}) collective-permute-start(bf16[128,128]{1,0:T(8,128)(2,1)S(1)} %collective-permute-done.3), channel_id=1, source_target_pairs={{0,15},{1,0},{2,1},{3,2},{4,3},{5,4},{6,5},{7,6},{8,7},{9,8},{10,9... | collective-permute-start | bytes 98312 | tf_op jit(solution)/shard_map/ppermute | solution.py:29
  30.9 1.9 collective-permute-start.6
  32.8 6.7 %collective-permute-start.7 = (bf16[128,128]{1,0:T(8,128)(2,1)S(1)}, bf16[128,128]{1,0:T(8,128)(2,1)S(1)}, u32[]{:S(2)}, u32[]{:S(2)}) collective-permute-start(bf16[128,128]{1,0:T(8,128)(2,1)S(1)} %collective-permute-done.5), channel_id=1, source_target_pairs={{0,15},{1,0},{2,1},{3,2},{4,3},{5,4},{6,5},{7,6},{8,7},{9,8},{10,9... | collective-permute-start | bytes 98312 | tf_op jit(solution)/shard_map/ppermute | solution.py:29
  39.6 1.9 collective-permute-start.8
  41.5 6.7 %collective-permute-start.9 = (bf16[128,128]{1,0:T(8,128)(2,1)S(1)}, bf16[128,128]{1,0:T(8,128)(2,1)S(1)}, u32[]{:S(2)}, u32[]{:S(2)}) collective-permute-start(bf16[128,128]{1,0:T(8,128)(2,1)S(1)} %collective-permute-done.7), channel_id=1, source_target_pairs={{0,15},{1,0},{2,1},{3,2},{4,3},{5,4},{6,5},{7,6},{8,7},{9,8},{10,9... | collective-permute-start | bytes 98312 | tf_op jit(solution)/shard_map/ppermute | solution.py:29
  48.3 1.9 collective-permute-start.10
  50.2 6.7 %collective-permute-start.11 = (bf16[128,128]{1,0:T(8,128)(2,1)S(1)}, bf16[128,128]{1,0:T(8,128)(2,1)S(1)}, u32[]{:S(2)}, u32[]{:S(2)}) collective-permute-start(bf16[128,128]{1,0:T(8,128)(2,1)S(1)} %collective-permute-done.9), channel_id=1, source_target_pairs={{0,15},{1,0},{2,1},{3,2},{4,3},{5,4},{6,5},{7,6},{8,7},{9,8},{10,9... | collective-permute-start | bytes 98312 | tf_op jit(solution)/shard_map/ppermute | solution.py:29
  56.9 1.9 collective-permute-start.12
  58.9 6.7 %collective-permute-start.13 = (bf16[128,128]{1,0:T(8,128)(2,1)S(1)}, bf16[128,128]{1,0:T(8,128)(2,1)S(1)}, u32[]{:S(2)}, u32[]{:S(2)}) collective-permute-start(bf16[128,128]{1,0:T(8,128)(2,1)S(1)} %collective-permute-done.11), channel_id=1, source_target_pairs={{0,15},{1,0},{2,1},{3,2},{4,3},{5,4},{6,5},{7,6},{8,7},{9,8},{10,9... | collective-permute-start | bytes 98312 | tf_op jit(solution)/shard_map/ppermute | solution.py:29
  65.6 1.9 collective-permute-start.14
  67.6 6.0 %collective-permute-done.14 = bf16[128,128]{1,0:T(8,128)(2,1)S(1)} collective-permute-done((bf16[128,128]{1,0:T(8,128)(2,1)S(1)}, bf16[128,128]{1,0:T(8,128)(2,1)S(1)}, u32[]{:S(2)}, u32[]{:S(2)}) %collective-permute-start.14) | collective-permute-done | bytes 32800 | tf_op jit(solution)/shard_map/ppermute | solution.py:22
  74.3 1.7 convolution_bitcast_fusion.3
  76.0 2.0 copy.43
  79.0 1.2 copy.44
  80.2 20.8 %all-to-all-start = ((f32[32,56,128]{2,1,0:T(8,128)}), f32[32,56,128]{2,1,0:T(8,128)S(1)}, u32[]{:S(2)}, u32[]{:S(2)}) async-start(f32[32,56,128]{2,1,0:T(8,128)} %bitcast.7), calls=%async_computation | async-start | bytes 1835008 | tf_op jit(solution)/shard_map/all_to_all | solution.py:45
  101.1 50.2 %all-to-all-done = f32[32,56,128]{2,1,0:T(8,128)S(1)} async-done(((f32[32,56,128]{2,1,0:T(8,128)}), f32[32,56,128]{2,1,0:T(8,128)S(1)}, u32[]{:S(2)}, u32[]{:S(2)}) %all-to-all-start) | async-done | bytes 917536 | tf_op jit(solution)/shard_map/all_to_all | solution.py:45
  151.3 29.7 %all_gather.9 = f32[1792,128]{1,0:T(8,128)S(1)} all-gather(f32[56,128]{1,0:T(8,128)S(1)} %reduce_sum.137), channel_id=1, replica_groups=mesh['comp'=32,'feat'=16] {'comp'}, dimensions={0}, use_global_device_ids=true | all-gather | bytes 946176 | tf_op jit(solution)/shard_map/all_gather | solution.py:110
  181.8 2.0 convolution_bitcast_fusion.2
  183.8 2.0 copy.46
  186.8 1.3 copy.47
  188.1 3.8 all-to-all-start.1
  191.9 17.4 %all-to-all-done.1 = f32[16,128,128]{2,1,0:T(8,128)S(1)} async-done(((f32[16,128,128]{2,1,0:T(8,128)}), f32[16,128,128]{2,1,0:T(8,128)S(1)}, u32[]{:S(2)}, u32[]{:S(2)}) %all-to-all-start.1) | async-done | bytes 1048608 | tf_op jit(solution)/shard_map/all_to_all | solution.py:45
  209.4 9.5 %all_to_all.45 = f32[16,2,128]{2,1,0:T(2,128)S(1)} all-to-all(f32[16,2,128]{2,1,0:T(2,128)S(1)} %broadcast_in_dim.30), channel_id=1, replica_groups=mesh['comp'=32,'feat'=16] {'feat'}, dimensions={0} | all-to-all | bytes 32768 | tf_op jit(solution)/shard_map/all_to_all | solution.py:50
  219.0 19.3 %all_to_all.46 = f32[32,2,128]{2,1,0:T(2,128)S(1)} all-to-all(f32[32,2,128]{2,1,0:T(2,128)S(1)} %broadcast_in_dim.31), channel_id=1, replica_groups=mesh['comp'=32,'feat'=16] {'comp'}, dimensions={0} | all-to-all | bytes 65536 | tf_op jit(solution)/shard_map/all_to_all | solution.py:52
  238.5 2.2 collective-permute-start.15
  240.7 6.4 %collective-permute-start.16 = (bf16[128,128]{1,0:T(8,128)(2,1)S(1)}, bf16[128,128]{1,0:T(8,128)(2,1)S(1)}, u32[]{:S(2)}, u32[]{:S(2)}) collective-permute-start(bf16[128,128]{1,0:T(8,128)(2,1)S(1)} %get-tuple-element.9), channel_id=1, source_target_pairs={{0,15},{1,0},{2,1},{3,2},{4,3},{5,4},{6,5},{7,6},{8,7},{9,8},{10,9... | collective-permute-start | bytes 98312 | tf_op jit(solution)/shard_map/ppermute | solution.py:29
  247.1 1.9 collective-permute-start.17
  249.1 6.7 %collective-permute-start.18 = (bf16[128,128]{1,0:T(8,128)(2,1)S(1)}, bf16[128,128]{1,0:T(8,128)(2,1)S(1)}, u32[]{:S(2)}, u32[]{:S(2)}) collective-permute-start(bf16[128,128]{1,0:T(8,128)(2,1)S(1)} %collective-permute-done.16), channel_id=1, source_target_pairs={{0,15},{1,0},{2,1},{3,2},{4,3},{5,4},{6,5},{7,6},{8,7},{9,8},{10,9... | collective-permute-start | bytes 98312 | tf_op jit(solution)/shard_map/ppermute | solution.py:29
  255.8 1.9 collective-permute-start.19
  257.8 6.7 %collective-permute-start.20 = (bf16[128,128]{1,0:T(8,128)(2,1)S(1)}, bf16[128,128]{1,0:T(8,128)(2,1)S(1)}, u32[]{:S(2)}, u32[]{:S(2)}) collective-permute-start(bf16[128,128]{1,0:T(8,128)(2,1)S(1)} %collective-permute-done.18), channel_id=1, source_target_pairs={{0,15},{1,0},{2,1},{3,2},{4,3},{5,4},{6,5},{7,6},{8,7},{9,8},{10,9... | collective-permute-start | bytes 98312 | tf_op jit(solution)/shard_map/ppermute | solution.py:29
  264.5 1.9 collective-permute-start.21
  266.5 6.7 %collective-permute-start.22 = (bf16[128,128]{1,0:T(8,128)(2,1)S(1)}, bf16[128,128]{1,0:T(8,128)(2,1)S(1)}, u32[]{:S(2)}, u32[]{:S(2)}) collective-permute-start(bf16[128,128]{1,0:T(8,128)(2,1)S(1)} %collective-permute-done.20), channel_id=1, source_target_pairs={{0,15},{1,0},{2,1},{3,2},{4,3},{5,4},{6,5},{7,6},{8,7},{9,8},{10,9... | collective-permute-start | bytes 98312 | tf_op jit(solution)/shard_map/ppermute | solution.py:29
  273.2 1.9 collective-permute-start.23
  275.1 6.7 %collective-permute-start.24 = (bf16[128,128]{1,0:T(8,128)(2,1)S(1)}, bf16[128,128]{1,0:T(8,128)(2,1)S(1)}, u32[]{:S(2)}, u32[]{:S(2)}) collective-permute-start(bf16[128,128]{1,0:T(8,128)(2,1)S(1)} %collective-permute-done.22), channel_id=1, source_target_pairs={{0,15},{1,0},{2,1},{3,2},{4,3},{5,4},{6,5},{7,6},{8,7},{9,8},{10,9... | collective-permute-start | bytes 98312 | tf_op jit(solution)/shard_map/ppermute | solution.py:29
  281.9 1.9 collective-permute-start.25
  283.8 6.7 %collective-permute-start.26 = (bf16[128,128]{1,0:T(8,128)(2,1)S(1)}, bf16[128,128]{1,0:T(8,128)(2,1)S(1)}, u32[]{:S(2)}, u32[]{:S(2)}) collective-permute-start(bf16[128,128]{1,0:T(8,128)(2,1)S(1)} %collective-permute-done.24), channel_id=1, source_target_pairs={{0,15},{1,0},{2,1},{3,2},{4,3},{5,4},{6,5},{7,6},{8,7},{9,8},{10,9... | collective-permute-start | bytes 98312 | tf_op jit(solution)/shard_map/ppermute | solution.py:29
  290.5 1.9 collective-permute-start.27
  292.5 6.7 %collective-permute-start.28 = (bf16[128,128]{1,0:T(8,128)(2,1)S(1)}, bf16[128,128]{1,0:T(8,128)(2,1)S(1)}, u32[]{:S(2)}, u32[]{:S(2)}) collective-permute-start(bf16[128,128]{1,0:T(8,128)(2,1)S(1)} %collective-permute-done.26), channel_id=1, source_target_pairs={{0,15},{1,0},{2,1},{3,2},{4,3},{5,4},{6,5},{7,6},{8,7},{9,8},{10,9... | collective-permute-start | bytes 98312 | tf_op jit(solution)/shard_map/ppermute | solution.py:29
  299.2 2.1 collective-permute-start.29
  301.4 5.8 %collective-permute-done.29 = bf16[128,128]{1,0:T(8,128)(2,1)S(1)} collective-permute-done((bf16[128,128]{1,0:T(8,128)(2,1)S(1)}, bf16[128,128]{1,0:T(8,128)(2,1)S(1)}, u32[]{:S(2)}, u32[]{:S(2)}) %collective-permute-start.29) | collective-permute-done | bytes 32800 | tf_op jit(solution)/shard_map/ppermute | solution.py:22
  307.9 1.7 convolution_bitcast_fusion.1
  309.6 2.0 copy.51
  311.5 1.0 fusion.23
  312.6 1.2 copy.52
  313.8 9.8 %all-to-all-start.4 = ((f32[32,56,128]{2,1,0:T(8,128)}), f32[32,56,128]{2,1,0:T(8,128)S(1)}, u32[]{:S(2)}, u32[]{:S(2)}) async-start(f32[32,56,128]{2,1,0:T(8,128)} %bitcast.17), calls=%async_computation.4 | async-start | bytes 1835008 | tf_op jit(solution)/shard_map/all_to_all | solution.py:45
  324.5 49.3 %all-to-all-done.4 = f32[32,56,128]{2,1,0:T(8,128)S(1)} async-done(((f32[32,56,128]{2,1,0:T(8,128)}), f32[32,56,128]{2,1,0:T(8,128)S(1)}, u32[]{:S(2)}, u32[]{:S(2)}) %all-to-all-start.4) | async-done | bytes 917536 | tf_op jit(solution)/shard_map/all_to_all | solution.py:45
  374.7 30.6 %all-gather.1 = f32[32,57,128]{2,1,0:T(8,128)S(1)} all-gather(f32[1,57,128]{2,1,0:T(8,128)S(1)} %maximum_bitcast_fusion), channel_id=2, replica_groups=mesh['comp'=32,'feat'=16] {'comp'}, dimensions={0}, use_global_device_ids=true | all-gather | bytes 963072 | tf_op jit(solution)/shard_map/all_gather | solution.py:120
  405.9 3.5 all-to-all-start.5
  410.4 5.3 %all-to-all-done.5 = f32[16,1,128]{2,1,0:T(1,128)S(1)} async-done(((f32[16,1,128]{2,1,0:T(1,128)}), f32[16,1,128]{2,1,0:T(1,128)S(1)}, u32[]{:S(2)}, u32[]{:S(2)}) %all-to-all-start.5) | async-done | bytes 8224 | tf_op jit(solution)/shard_map/all_to_all | solution.py:129
  415.7 2.2 fusion.53
  418.6 2.0 convolution_bitcast_fusion
  420.6 2.0 copy.55
  422.6 1.0 fusion.17
  423.6 1.3 copy.56
  424.9 3.7 all-to-all-start.6
  429.3 14.5 %all-to-all-done.6 = f32[16,128,128]{2,1,0:T(8,128)S(1)} async-done(((f32[16,128,128]{2,1,0:T(8,128)}), f32[16,128,128]{2,1,0:T(8,128)S(1)}, u32[]{:S(2)}, u32[]{:S(2)}) %all-to-all-start.6) | async-done | bytes 1048608 | tf_op jit(solution)/shard_map/all_to_all | solution.py:45
  443.9 10.1 %all_to_all.47 = f32[16,2,128]{2,1,0:T(2,128)S(1)} all-to-all(f32[16,2,128]{2,1,0:T(2,128)S(1)} %broadcast_in_dim.34), channel_id=1, replica_groups=mesh['comp'=32,'feat'=16] {'feat'}, dimensions={0} | all-to-all | bytes 32768 | tf_op jit(solution)/shard_map/all_to_all | solution.py:50
  454.1 19.7 %all_to_all.48 = f32[32,2,128]{2,1,0:T(2,128)S(1)} all-to-all(f32[32,2,128]{2,1,0:T(2,128)S(1)} %broadcast_in_dim.35), channel_id=1, replica_groups=mesh['comp'=32,'feat'=16] {'comp'}, dimensions={0} | all-to-all | bytes 65536 | tf_op jit(solution)/shard_map/all_to_all | solution.py:52
  473.9 2.2 multiply_add_fusion
  (114 shorter events, 13.3 us)
Async XLA Ops:
  0.6 73.7 %copy-start = (bf16[1,1,24,128,128]{4,3,2,1,0:T(8,128)(2,1)S(1)}, bf16[1,1,24,128,128]{4,3,2,1,0:T(8,128)(2,1)}, u32[]{:S(2)}) copy-start(bf16[1,1,24,128,128]{4,3,2,1,0:T(8,128)(2,1)} %param.10) | copy-start | bytes 2359300
  1.6 11.9 %collective-permute-start = (bf16[128,128]{1,0:T(8,128)(2,1)S(1)}, bf16[128,128]{1,0:T(8,128)(2,1)S(1)}, u32[]{:S(2)}, u32[]{:S(2)}) collective-permute-start(bf16[128,128]{1,0:T(8,128)(2,1)S(1)} %get-tuple-element.11), channel_id=1, source_target_pairs={{0,1},{1,2},{2,3},{3,4},{4,5},{5,6},{6,7},{7,8},{8,9},{9,10},{10,1... | collective-permute-start | bytes 98312 | tf_op jit(solution)/shard_map/ppermute | solution.py:22
  5.7 9.8 %collective-permute-start.1 = (bf16[128,128]{1,0:T(8,128)(2,1)S(1)}, bf16[128,128]{1,0:T(8,128)(2,1)S(1)}, u32[]{:S(2)}, u32[]{:S(2)}) collective-permute-start(bf16[128,128]{1,0:T(8,128)(2,1)S(1)} %get-tuple-element.11), channel_id=1, source_target_pairs={{0,15},{1,0},{2,1},{3,2},{4,3},{5,4},{6,5},{7,6},{8,7},{9,8},{10,9... | collective-permute-start | bytes 98312 | tf_op jit(solution)/shard_map/ppermute | solution.py:29
  13.5 8.7 %collective-permute-start.2 = (bf16[128,128]{1,0:T(8,128)(2,1)S(1)}, bf16[128,128]{1,0:T(8,128)(2,1)S(1)}, u32[]{:S(2)}, u32[]{:S(2)}) collective-permute-start(bf16[128,128]{1,0:T(8,128)(2,1)S(1)} %collective-permute-done), channel_id=1, source_target_pairs={{0,1},{1,2},{2,3},{3,4},{4,5},{5,6},{6,7},{7,8},{8,9},{9,10},{10,1... | collective-permute-start | bytes 98312 | tf_op jit(solution)/shard_map/ppermute | solution.py:22
  15.5 8.7 %collective-permute-start.3 = (bf16[128,128]{1,0:T(8,128)(2,1)S(1)}, bf16[128,128]{1,0:T(8,128)(2,1)S(1)}, u32[]{:S(2)}, u32[]{:S(2)}) collective-permute-start(bf16[128,128]{1,0:T(8,128)(2,1)S(1)} %collective-permute-done.1), channel_id=1, source_target_pairs={{0,15},{1,0},{2,1},{3,2},{4,3},{5,4},{6,5},{7,6},{8,7},{9,8},{10,9... | collective-permute-start | bytes 98312 | tf_op jit(solution)/shard_map/ppermute | solution.py:29
  22.2 8.7 %collective-permute-start.4 = (bf16[128,128]{1,0:T(8,128)(2,1)S(1)}, bf16[128,128]{1,0:T(8,128)(2,1)S(1)}, u32[]{:S(2)}, u32[]{:S(2)}) collective-permute-start(bf16[128,128]{1,0:T(8,128)(2,1)S(1)} %collective-permute-done.2), channel_id=1, source_target_pairs={{0,1},{1,2},{2,3},{3,4},{4,5},{5,6},{6,7},{7,8},{8,9},{9,10},{10,1... | collective-permute-start | bytes 98312 | tf_op jit(solution)/shard_map/ppermute | solution.py:22
  24.2 8.7 %collective-permute-start.5 = (bf16[128,128]{1,0:T(8,128)(2,1)S(1)}, bf16[128,128]{1,0:T(8,128)(2,1)S(1)}, u32[]{:S(2)}, u32[]{:S(2)}) collective-permute-start(bf16[128,128]{1,0:T(8,128)(2,1)S(1)} %collective-permute-done.3), channel_id=1, source_target_pairs={{0,15},{1,0},{2,1},{3,2},{4,3},{5,4},{6,5},{7,6},{8,7},{9,8},{10,9... | collective-permute-start | bytes 98312 | tf_op jit(solution)/shard_map/ppermute | solution.py:29
  30.9 8.7 %collective-permute-start.6 = (bf16[128,128]{1,0:T(8,128)(2,1)S(1)}, bf16[128,128]{1,0:T(8,128)(2,1)S(1)}, u32[]{:S(2)}, u32[]{:S(2)}) collective-permute-start(bf16[128,128]{1,0:T(8,128)(2,1)S(1)} %collective-permute-done.4), channel_id=1, source_target_pairs={{0,1},{1,2},{2,3},{3,4},{4,5},{5,6},{6,7},{7,8},{8,9},{9,10},{10,1... | collective-permute-start | bytes 98312 | tf_op jit(solution)/shard_map/ppermute | solution.py:22
  32.8 8.7 %collective-permute-start.7 = (bf16[128,128]{1,0:T(8,128)(2,1)S(1)}, bf16[128,128]{1,0:T(8,128)(2,1)S(1)}, u32[]{:S(2)}, u32[]{:S(2)}) collective-permute-start(bf16[128,128]{1,0:T(8,128)(2,1)S(1)} %collective-permute-done.5), channel_id=1, source_target_pairs={{0,15},{1,0},{2,1},{3,2},{4,3},{5,4},{6,5},{7,6},{8,7},{9,8},{10,9... | collective-permute-start | bytes 98312 | tf_op jit(solution)/shard_map/ppermute | solution.py:29
  39.6 8.7 %collective-permute-start.8 = (bf16[128,128]{1,0:T(8,128)(2,1)S(1)}, bf16[128,128]{1,0:T(8,128)(2,1)S(1)}, u32[]{:S(2)}, u32[]{:S(2)}) collective-permute-start(bf16[128,128]{1,0:T(8,128)(2,1)S(1)} %collective-permute-done.6), channel_id=1, source_target_pairs={{0,1},{1,2},{2,3},{3,4},{4,5},{5,6},{6,7},{7,8},{8,9},{9,10},{10,1... | collective-permute-start | bytes 98312 | tf_op jit(solution)/shard_map/ppermute | solution.py:22
  41.5 8.7 %collective-permute-start.9 = (bf16[128,128]{1,0:T(8,128)(2,1)S(1)}, bf16[128,128]{1,0:T(8,128)(2,1)S(1)}, u32[]{:S(2)}, u32[]{:S(2)}) collective-permute-start(bf16[128,128]{1,0:T(8,128)(2,1)S(1)} %collective-permute-done.7), channel_id=1, source_target_pairs={{0,15},{1,0},{2,1},{3,2},{4,3},{5,4},{6,5},{7,6},{8,7},{9,8},{10,9... | collective-permute-start | bytes 98312 | tf_op jit(solution)/shard_map/ppermute | solution.py:29
  48.3 8.7 %collective-permute-start.10 = (bf16[128,128]{1,0:T(8,128)(2,1)S(1)}, bf16[128,128]{1,0:T(8,128)(2,1)S(1)}, u32[]{:S(2)}, u32[]{:S(2)}) collective-permute-start(bf16[128,128]{1,0:T(8,128)(2,1)S(1)} %collective-permute-done.8), channel_id=1, source_target_pairs={{0,1},{1,2},{2,3},{3,4},{4,5},{5,6},{6,7},{7,8},{8,9},{9,10},{10,1... | collective-permute-start | bytes 98312 | tf_op jit(solution)/shard_map/ppermute | solution.py:22
  50.2 8.7 %collective-permute-start.11 = (bf16[128,128]{1,0:T(8,128)(2,1)S(1)}, bf16[128,128]{1,0:T(8,128)(2,1)S(1)}, u32[]{:S(2)}, u32[]{:S(2)}) collective-permute-start(bf16[128,128]{1,0:T(8,128)(2,1)S(1)} %collective-permute-done.9), channel_id=1, source_target_pairs={{0,15},{1,0},{2,1},{3,2},{4,3},{5,4},{6,5},{7,6},{8,7},{9,8},{10,9... | collective-permute-start | bytes 98312 | tf_op jit(solution)/shard_map/ppermute | solution.py:29
  56.9 8.7 %collective-permute-start.12 = (bf16[128,128]{1,0:T(8,128)(2,1)S(1)}, bf16[128,128]{1,0:T(8,128)(2,1)S(1)}, u32[]{:S(2)}, u32[]{:S(2)}) collective-permute-start(bf16[128,128]{1,0:T(8,128)(2,1)S(1)} %collective-permute-done.10), channel_id=1, source_target_pairs={{0,1},{1,2},{2,3},{3,4},{4,5},{5,6},{6,7},{7,8},{8,9},{9,10},{10,1... | collective-permute-start | bytes 98312 | tf_op jit(solution)/shard_map/ppermute | solution.py:22
  58.9 8.7 %collective-permute-start.13 = (bf16[128,128]{1,0:T(8,128)(2,1)S(1)}, bf16[128,128]{1,0:T(8,128)(2,1)S(1)}, u32[]{:S(2)}, u32[]{:S(2)}) collective-permute-start(bf16[128,128]{1,0:T(8,128)(2,1)S(1)} %collective-permute-done.11), channel_id=1, source_target_pairs={{0,15},{1,0},{2,1},{3,2},{4,3},{5,4},{6,5},{7,6},{8,7},{9,8},{10,9... | collective-permute-start | bytes 98312 | tf_op jit(solution)/shard_map/ppermute | solution.py:29
  65.6 8.0 %collective-permute-start.14 = (bf16[128,128]{1,0:T(8,128)(2,1)S(1)}, bf16[128,128]{1,0:T(8,128)(2,1)S(1)}, u32[]{:S(2)}, u32[]{:S(2)}) collective-permute-start(bf16[128,128]{1,0:T(8,128)(2,1)S(1)} %collective-permute-done.12), channel_id=1, source_target_pairs={{0,1},{1,2},{2,3},{3,4},{4,5},{5,6},{6,7},{7,8},{8,9},{9,10},{10,1... | collective-permute-start | bytes 98312 | tf_op jit(solution)/shard_map/ppermute | solution.py:22
  76.0 2.0 copy-start.2
  80.2 71.0 %all-to-all-start = ((f32[32,56,128]{2,1,0:T(8,128)}), f32[32,56,128]{2,1,0:T(8,128)S(1)}, u32[]{:S(2)}, u32[]{:S(2)}) async-start(f32[32,56,128]{2,1,0:T(8,128)} %bitcast.7), calls=%async_computation | async-start | bytes 1835008 | tf_op jit(solution)/shard_map/all_to_all | solution.py:45
  183.8 2.0 copy-start.3
  188.1 50.3 %copy-start.4 = (f32[128]{0:T(128)S(1)}, f32[128]{0:T(128)}, u32[]{:S(2)}) copy-start(f32[128]{0:T(128)} %param.15) | copy-start | bytes 1540
  188.1 50.4 %copy-start.1 = (f32[128,128]{1,0:T(8,128)S(1)}, f32[128,128]{1,0:T(8,128)}, u32[]{:S(2)}) copy-start(f32[128,128]{1,0:T(8,128)} %param.14) | copy-start | bytes 196612
  188.1 21.2 %all-to-all-start.1 = ((f32[16,128,128]{2,1,0:T(8,128)}), f32[16,128,128]{2,1,0:T(8,128)S(1)}, u32[]{:S(2)}, u32[]{:S(2)}) async-start(f32[16,128,128]{2,1,0:T(8,128)} %copy.47), calls=%async_computation.1 | async-start | bytes 2097152 | tf_op jit(solution)/shard_map/all_to_all | solution.py:45
  238.5 8.6 %collective-permute-start.15 = (bf16[128,128]{1,0:T(8,128)(2,1)S(1)}, bf16[128,128]{1,0:T(8,128)(2,1)S(1)}, u32[]{:S(2)}, u32[]{:S(2)}) collective-permute-start(bf16[128,128]{1,0:T(8,128)(2,1)S(1)} %get-tuple-element.9), channel_id=1, source_target_pairs={{0,1},{1,2},{2,3},{3,4},{4,5},{5,6},{6,7},{7,8},{8,9},{9,10},{10,1... | collective-permute-start | bytes 98312 | tf_op jit(solution)/shard_map/ppermute | solution.py:22
  240.7 8.4 %collective-permute-start.16 = (bf16[128,128]{1,0:T(8,128)(2,1)S(1)}, bf16[128,128]{1,0:T(8,128)(2,1)S(1)}, u32[]{:S(2)}, u32[]{:S(2)}) collective-permute-start(bf16[128,128]{1,0:T(8,128)(2,1)S(1)} %get-tuple-element.9), channel_id=1, source_target_pairs={{0,15},{1,0},{2,1},{3,2},{4,3},{5,4},{6,5},{7,6},{8,7},{9,8},{10,9... | collective-permute-start | bytes 98312 | tf_op jit(solution)/shard_map/ppermute | solution.py:29
  247.1 8.7 %collective-permute-start.17 = (bf16[128,128]{1,0:T(8,128)(2,1)S(1)}, bf16[128,128]{1,0:T(8,128)(2,1)S(1)}, u32[]{:S(2)}, u32[]{:S(2)}) collective-permute-start(bf16[128,128]{1,0:T(8,128)(2,1)S(1)} %collective-permute-done.15), channel_id=1, source_target_pairs={{0,1},{1,2},{2,3},{3,4},{4,5},{5,6},{6,7},{7,8},{8,9},{9,10},{10,1... | collective-permute-start | bytes 98312 | tf_op jit(solution)/shard_map/ppermute | solution.py:22
  249.1 8.7 %collective-permute-start.18 = (bf16[128,128]{1,0:T(8,128)(2,1)S(1)}, bf16[128,128]{1,0:T(8,128)(2,1)S(1)}, u32[]{:S(2)}, u32[]{:S(2)}) collective-permute-start(bf16[128,128]{1,0:T(8,128)(2,1)S(1)} %collective-permute-done.16), channel_id=1, source_target_pairs={{0,15},{1,0},{2,1},{3,2},{4,3},{5,4},{6,5},{7,6},{8,7},{9,8},{10,9... | collective-permute-start | bytes 98312 | tf_op jit(solution)/shard_map/ppermute | solution.py:29
  255.8 8.7 %collective-permute-start.19 = (bf16[128,128]{1,0:T(8,128)(2,1)S(1)}, bf16[128,128]{1,0:T(8,128)(2,1)S(1)}, u32[]{:S(2)}, u32[]{:S(2)}) collective-permute-start(bf16[128,128]{1,0:T(8,128)(2,1)S(1)} %collective-permute-done.17), channel_id=1, source_target_pairs={{0,1},{1,2},{2,3},{3,4},{4,5},{5,6},{6,7},{7,8},{8,9},{9,10},{10,1... | collective-permute-start | bytes 98312 | tf_op jit(solution)/shard_map/ppermute | solution.py:22
  257.8 8.7 %collective-permute-start.20 = (bf16[128,128]{1,0:T(8,128)(2,1)S(1)}, bf16[128,128]{1,0:T(8,128)(2,1)S(1)}, u32[]{:S(2)}, u32[]{:S(2)}) collective-permute-start(bf16[128,128]{1,0:T(8,128)(2,1)S(1)} %collective-permute-done.18), channel_id=1, source_target_pairs={{0,15},{1,0},{2,1},{3,2},{4,3},{5,4},{6,5},{7,6},{8,7},{9,8},{10,9... | collective-permute-start | bytes 98312 | tf_op jit(solution)/shard_map/ppermute | solution.py:29
  264.5 8.7 %collective-permute-start.21 = (bf16[128,128]{1,0:T(8,128)(2,1)S(1)}, bf16[128,128]{1,0:T(8,128)(2,1)S(1)}, u32[]{:S(2)}, u32[]{:S(2)}) collective-permute-start(bf16[128,128]{1,0:T(8,128)(2,1)S(1)} %collective-permute-done.19), channel_id=1, source_target_pairs={{0,1},{1,2},{2,3},{3,4},{4,5},{5,6},{6,7},{7,8},{8,9},{9,10},{10,1... | collective-permute-start | bytes 98312 | tf_op jit(solution)/shard_map/ppermute | solution.py:22
  266.5 8.7 %collective-permute-start.22 = (bf16[128,128]{1,0:T(8,128)(2,1)S(1)}, bf16[128,128]{1,0:T(8,128)(2,1)S(1)}, u32[]{:S(2)}, u32[]{:S(2)}) collective-permute-start(bf16[128,128]{1,0:T(8,128)(2,1)S(1)} %collective-permute-done.20), channel_id=1, source_target_pairs={{0,15},{1,0},{2,1},{3,2},{4,3},{5,4},{6,5},{7,6},{8,7},{9,8},{10,9... | collective-permute-start | bytes 98312 | tf_op jit(solution)/shard_map/ppermute | solution.py:29
  273.2 8.7 %collective-permute-start.23 = (bf16[128,128]{1,0:T(8,128)(2,1)S(1)}, bf16[128,128]{1,0:T(8,128)(2,1)S(1)}, u32[]{:S(2)}, u32[]{:S(2)}) collective-permute-start(bf16[128,128]{1,0:T(8,128)(2,1)S(1)} %collective-permute-done.21), channel_id=1, source_target_pairs={{0,1},{1,2},{2,3},{3,4},{4,5},{5,6},{6,7},{7,8},{8,9},{9,10},{10,1... | collective-permute-start | bytes 98312 | tf_op jit(solution)/shard_map/ppermute | solution.py:22
  275.1 8.7 %collective-permute-start.24 = (bf16[128,128]{1,0:T(8,128)(2,1)S(1)}, bf16[128,128]{1,0:T(8,128)(2,1)S(1)}, u32[]{:S(2)}, u32[]{:S(2)}) collective-permute-start(bf16[128,128]{1,0:T(8,128)(2,1)S(1)} %collective-permute-done.22), channel_id=1, source_target_pairs={{0,15},{1,0},{2,1},{3,2},{4,3},{5,4},{6,5},{7,6},{8,7},{9,8},{10,9... | collective-permute-start | bytes 98312 | tf_op jit(solution)/shard_map/ppermute | solution.py:29
  281.9 8.7 %collective-permute-start.25 = (bf16[128,128]{1,0:T(8,128)(2,1)S(1)}, bf16[128,128]{1,0:T(8,128)(2,1)S(1)}, u32[]{:S(2)}, u32[]{:S(2)}) collective-permute-start(bf16[128,128]{1,0:T(8,128)(2,1)S(1)} %collective-permute-done.23), channel_id=1, source_target_pairs={{0,1},{1,2},{2,3},{3,4},{4,5},{5,6},{6,7},{7,8},{8,9},{9,10},{10,1... | collective-permute-start | bytes 98312 | tf_op jit(solution)/shard_map/ppermute | solution.py:22
  283.8 8.7 %collective-permute-start.26 = (bf16[128,128]{1,0:T(8,128)(2,1)S(1)}, bf16[128,128]{1,0:T(8,128)(2,1)S(1)}, u32[]{:S(2)}, u32[]{:S(2)}) collective-permute-start(bf16[128,128]{1,0:T(8,128)(2,1)S(1)} %collective-permute-done.24), channel_id=1, source_target_pairs={{0,15},{1,0},{2,1},{3,2},{4,3},{5,4},{6,5},{7,6},{8,7},{9,8},{10,9... | collective-permute-start | bytes 98312 | tf_op jit(solution)/shard_map/ppermute | solution.py:29
  290.5 8.7 %collective-permute-start.27 = (bf16[128,128]{1,0:T(8,128)(2,1)S(1)}, bf16[128,128]{1,0:T(8,128)(2,1)S(1)}, u32[]{:S(2)}, u32[]{:S(2)}) collective-permute-start(bf16[128,128]{1,0:T(8,128)(2,1)S(1)} %collective-permute-done.25), channel_id=1, source_target_pairs={{0,1},{1,2},{2,3},{3,4},{4,5},{5,6},{6,7},{7,8},{8,9},{9,10},{10,1... | collective-permute-start | bytes 98312 | tf_op jit(solution)/shard_map/ppermute | solution.py:22
  292.5 8.9 %collective-permute-start.28 = (bf16[128,128]{1,0:T(8,128)(2,1)S(1)}, bf16[128,128]{1,0:T(8,128)(2,1)S(1)}, u32[]{:S(2)}, u32[]{:S(2)}) collective-permute-start(bf16[128,128]{1,0:T(8,128)(2,1)S(1)} %collective-permute-done.26), channel_id=1, source_target_pairs={{0,15},{1,0},{2,1},{3,2},{4,3},{5,4},{6,5},{7,6},{8,7},{9,8},{10,9... | collective-permute-start | bytes 98312 | tf_op jit(solution)/shard_map/ppermute | solution.py:29
  299.2 8.0 %collective-permute-start.29 = (bf16[128,128]{1,0:T(8,128)(2,1)S(1)}, bf16[128,128]{1,0:T(8,128)(2,1)S(1)}, u32[]{:S(2)}, u32[]{:S(2)}) collective-permute-start(bf16[128,128]{1,0:T(8,128)(2,1)S(1)} %collective-permute-done.27), channel_id=1, source_target_pairs={{0,1},{1,2},{2,3},{3,4},{4,5},{5,6},{6,7},{7,8},{8,9},{9,10},{10,1... | collective-permute-start | bytes 98312 | tf_op jit(solution)/shard_map/ppermute | solution.py:22
  313.8 60.0 %all-to-all-start.4 = ((f32[32,56,128]{2,1,0:T(8,128)}), f32[32,56,128]{2,1,0:T(8,128)S(1)}, u32[]{:S(2)}, u32[]{:S(2)}) async-start(f32[32,56,128]{2,1,0:T(8,128)} %bitcast.17), calls=%async_computation.4 | async-start | bytes 1835008 | tf_op jit(solution)/shard_map/all_to_all | solution.py:45
  405.9 9.8 %all-to-all-start.5 = ((f32[16,1,128]{2,1,0:T(1,128)}), f32[16,1,128]{2,1,0:T(1,128)S(1)}, u32[]{:S(2)}, u32[]{:S(2)}) async-start(f32[16,1,128]{2,1,0:T(1,128)} %broadcast_in_dim.33), calls=%async_computation.5 | async-start | bytes 16384 | tf_op jit(solution)/shard_map/all_to_all | solution.py:129
  424.9 18.9 %all-to-all-start.6 = ((f32[16,128,128]{2,1,0:T(8,128)}), f32[16,128,128]{2,1,0:T(8,128)S(1)}, u32[]{:S(2)}, u32[]{:S(2)}) async-start(f32[16,128,128]{2,1,0:T(8,128)} %copy.56), calls=%async_computation.6 | async-start | bytes 2097152 | tf_op jit(solution)/shard_map/all_to_all | solution.py:45
